TPU v7x, 128 devices: a whole 4x4x4 slice. The times are simulated.
128 devices in a mesh: node: 8 (over x, core), dev: 16 (over z, y).
Axes of the slice: x: 4, y: 4, z: 4, core: 2. Of those that a mesh axis runs over, the one named last changes fastest.
Arguments:
- tokens: bfloat16 [32768, 7168], P(('node', 'dev')), may hold values from -6 to 6
- grad_out: bfloat16 [32768, 7168], P(('node', 'dev')), may hold values from -1.796875 to 1.796875
- router_gates: bfloat16 [32768, 8], P(('node', 'dev')), may hold values from 0.049804688 to 1
- expert_ids: int32 [32768, 8], P(('node', 'dev')), may hold values from 0 to 255, as said below
- slot_plan: int32 [256, 2], replicated, may hold values from 0 to 16, as said below
- w_gate: bfloat16 [8, 7168, 2048], P(None, 'dev', 'node'), may hold values from -0.0625 to 0.0625
- w_up: bfloat16 [8, 7168, 2048], P(None, 'dev', 'node'), may hold values from -0.0625 to 0.0625
- w_down: bfloat16 [8, 2048, 7168], P(None, 'node', 'dev'), may hold values from -0.125 to 0.125
Outputs:
- grad_tokens: bfloat16 [32768, 7168], P(('node', 'dev'))
- grad_gates: float32 [32768, 8], P(('node', 'dev'))
- grad_w_gate: bfloat16 [8, 7168, 2048], P(None, 'dev', 'node')
- grad_w_up: bfloat16 [8, 7168, 2048], P(None, 'dev', 'node')
- grad_w_down: bfloat16 [8, 2048, 7168], P(None, 'node', 'dev')
Inputs may be any that keep to these rules, and one draw needn't show every extreme that they name: `expert_ids`: each token names 8 different experts. Within one block of 256 tokens (the tokens of one device), at most 4 pairs name any one expert that has slots, and in every draw one expert that has slots is named exactly 2 * 2 times in every block. `slot_plan`: exactly 8 rows hold slots: each such row holds two different slots, and every slot 0 .. 15 stands in exactly one row. Every entry of the other rows equals 16.
All inputs are finite; a program needn't handle non-finite values.
Results may differ from a plain program's by a relative error of at most 0.0059.
Values may be sent and summed in bfloat16 or wider, within the bound.
No kernel may reach another device: no remote copies, remote signals or barrier semaphores. Data moves between devices by JAX's collectives and lax.ppermute only.
A program may use at most 128 MiB of HBM per device.

v0:
```python
import jax
import jax.numpy as jnp
from jax import lax
from jax.sharding import PartitionSpec as P

TOP = 8
CAP = 2
REPS = 2
LANE = 128


def routing(expert_ids, slot_plan, slot_count, round_total):
    expert_count = slot_plan.shape[0]
    in_round = (slot_plan[:, 0] < slot_count).astype(jnp.int32)
    expert_rank = jnp.cumsum(in_round) - 1
    rank_match = (in_round[:, None] > 0) & (
        expert_rank[:, None] == jnp.arange(round_total, dtype=jnp.int32)[None, :]
    )
    hot_ids = jnp.sum(
        jnp.where(rank_match, jnp.arange(expert_count, dtype=jnp.int32)[:, None], 0), axis=0
    )
    match = expert_ids[:, :, None] == hot_ids[None, None, :]
    named = jnp.sum(match.astype(jnp.int32), axis=1)
    tok_rows = expert_ids.shape[0]
    earlier = (
        jnp.arange(tok_rows, dtype=jnp.int32)[None, :]
        < jnp.arange(tok_rows, dtype=jnp.int32)[:, None]
    ).astype(jnp.bfloat16)
    before = jnp.dot(
        earlier, named.astype(jnp.bfloat16), preferred_element_type=jnp.float32
    ).astype(jnp.int32)
    per_rank = REPS * CAP
    target = per_rank * jnp.arange(round_total, dtype=jnp.int32)[None, :] + before
    return (match, named, target)


def local(tokens, grad_out, router_gates, expert_ids, slot_plan, w_gate, w_up, w_down):
    col_count = lax.axis_size("dev")
    node_count = lax.axis_size("node")
    tok_rows, model_width = tokens.shape
    round_total, chunk, node_hidden = w_gate.shape
    half = node_hidden // REPS
    per_rank = REPS * CAP
    row_slots = round_total * per_rank
    wide = model_width + LANE

    def split_cols(w):
        w = w.reshape(round_total, chunk, REPS, half)
        return jnp.swapaxes(w, 1, 2).reshape(col_count, chunk, half)

    send_wg = split_cols(w_gate)
    send_wu = split_cols(w_up)
    send_wd = split_cols(jnp.swapaxes(w_down, 1, 2))
    slot_gate = lax.all_to_all(send_wg, "dev", 0, 0, tiled=True).reshape(model_width, half)
    slot_up = lax.all_to_all(send_wu, "dev", 0, 0, tiled=True).reshape(model_width, half)
    slot_down_t = lax.all_to_all(send_wd, "dev", 0, 0, tiled=True).reshape(model_width, half)
    match, named, target = routing(expert_ids, slot_plan, col_count, round_total)
    q_ids = jnp.arange(row_slots, dtype=jnp.int32)
    chooser = (named[None, :, :] > 0) & (target[None, :, :] == q_ids[:, None, None])
    pick_rows = jnp.sum(chooser.astype(jnp.float32), axis=-1)
    pick_half = pick_rows.astype(jnp.bfloat16)
    gates_f = router_gates.astype(jnp.float32)
    rank_gate = jnp.sum(jnp.where(match, gates_f[:, :, None], 0.0), axis=1)
    gate_send = jnp.sum(jnp.where(chooser, rank_gate[None, :, :], 0.0), axis=(1, 2)).astype(
        jnp.bfloat16
    )
    x_send = jnp.dot(pick_half, tokens, preferred_element_type=jnp.float32).astype(jnp.bfloat16)
    dy_send = jnp.dot(pick_half, grad_out, preferred_element_type=jnp.float32).astype(jnp.bfloat16)
    gate_block = jnp.where(
        jnp.arange(LANE)[None, :] == 0, gate_send[:, None], jnp.zeros((), jnp.bfloat16)
    )
    dy_send = jnp.concatenate([dy_send, gate_block], axis=1)
    both_send = jnp.concatenate([x_send, dy_send], axis=1)
    both_width = model_width + wide
    both = both_send.reshape(round_total, 1, per_rank, both_width)
    both = jnp.broadcast_to(both, (round_total, REPS, per_rank, both_width))
    both = lax.all_to_all(both.reshape(col_count, per_rank, both_width), "dev", 0, 0, tiled=True)
    both = both.reshape(col_count * per_rank, both_width)
    x_rows = lax.all_gather(both[:, :model_width], "node", axis=0, tiled=True)
    dy_ext = lax.all_gather(both[:, model_width:], "node", axis=0, tiled=True)
    dy_rows = dy_ext[:, :model_width]
    gate_rows = dy_ext[:, model_width].astype(jnp.float32)[:, None]
    gate_pre = jnp.dot(x_rows, slot_gate, preferred_element_type=jnp.float32)
    up_pre = jnp.dot(x_rows, slot_up, preferred_element_type=jnp.float32)
    back_proj = jnp.dot(dy_rows, slot_down_t, preferred_element_type=jnp.float32)
    sigmoid_gate = jax.nn.sigmoid(gate_pre)
    active = gate_pre * sigmoid_gate
    hidden = active * up_pre
    scaled_back = gate_rows * back_proj
    d_gate = (scaled_back * up_pre * sigmoid_gate * (1.0 + gate_pre * (1.0 - sigmoid_gate))).astype(
        jnp.bfloat16
    )
    d_up = (scaled_back * active).astype(jnp.bfloat16)
    scaled_hidden = (gate_rows * hidden).astype(jnp.bfloat16)
    gate_terms = jnp.sum(back_proj * hidden, axis=-1)
    row_count = x_rows.shape[0]
    first_slot = (jnp.arange(row_count, dtype=jnp.int32) % REPS == 0)[:, None]

    def by_slot(d):
        zero = jnp.zeros((), d.dtype)
        return jnp.concatenate(
            [jnp.where(first_slot, d, zero), jnp.where(first_slot, zero, d)], axis=1
        )

    def slot_pair_sum(rows, d):
        acc = jnp.einsum("rd,rh->dh", rows, by_slot(d), preferred_element_type=jnp.float32)
        acc = lax.reduce_precision(acc, exponent_bits=8, mantissa_bits=7)
        return (acc[:, :half] + acc[:, half:]).astype(jnp.bfloat16)

    grad_gate_cols = slot_pair_sum(x_rows, d_gate)
    grad_up_cols = slot_pair_sum(x_rows, d_up)
    grad_down_cols = slot_pair_sum(dy_rows, scaled_hidden)
    pad_rows = ((0, LANE), (0, 0))
    row_ext = jnp.einsum(
        "rh,dh->rd", d_gate, jnp.pad(slot_gate, pad_rows), preferred_element_type=jnp.float32
    )
    row_ext = row_ext + jnp.einsum(
        "rh,dh->rd", d_up, jnp.pad(slot_up, pad_rows), preferred_element_type=jnp.float32
    )
    term_col = jnp.arange(wide, dtype=jnp.int32)[None, :] == model_width
    row_ext = row_ext + jnp.where(term_col, gate_terms[:, None], 0.0)
    summed = lax.psum_scatter(row_ext, "node", scatter_dimension=0, tiled=True)
    back = lax.all_to_all(summed.reshape(col_count, per_rank, wide), "dev", 0, 0, tiled=True)
    back = jnp.sum(back.reshape(round_total, REPS, per_rank, wide), axis=1).reshape(row_slots, wide)
    back_tok = back[:, :model_width]
    back_hi = back_tok.astype(jnp.bfloat16)
    back_lo = (back_tok - back_hi.astype(jnp.float32)).astype(jnp.bfloat16)
    grad_tokens = jnp.einsum("qt,qd->td", pick_half, back_hi, preferred_element_type=jnp.float32)
    grad_tokens = grad_tokens + jnp.einsum(
        "qt,qd->td", pick_half, back_lo, preferred_element_type=jnp.float32
    )
    grad_tokens = grad_tokens.astype(jnp.bfloat16)
    back_q = back[:, model_width]
    rank_back = jnp.sum(jnp.where(chooser, back_q[:, None, None], 0.0), axis=0)
    grad_gates = jnp.sum(jnp.where(match, rank_back[:, None, :], 0.0), axis=-1)

    def home(cols):
        sent = cols.reshape(col_count, chunk, half)
        got = lax.all_to_all(sent, "dev", 0, 0, tiled=True).reshape(round_total, REPS, chunk, half)
        return jnp.concatenate([got[:, h] for h in range(REPS)], axis=-1)

    grad_w_gate = home(grad_gate_cols)
    grad_w_up = home(grad_up_cols)
    got_down = lax.all_to_all(
        grad_down_cols.reshape(col_count, chunk, half), "dev", 0, 0, tiled=True
    )
    got_down = got_down.reshape(round_total, REPS, chunk, half)
    grad_w_down = jnp.concatenate([jnp.swapaxes(got_down[:, h], 1, 2) for h in range(REPS)], axis=1)
    del node_count
    return (grad_tokens, grad_gates, grad_w_gate, grad_w_up, grad_w_down)


def solution(mesh):
    return jax.shard_map(
        local,
        mesh=mesh,
        in_specs=(
            P(("node", "dev"), None),
            P(("node", "dev"), None),
            P(("node", "dev"), None),
            P(("node", "dev"), None),
            P(),
            P(None, "dev", "node"),
            P(None, "dev", "node"),
            P(None, "node", "dev"),
        ),
        out_specs=(
            P(("node", "dev"), None),
            P(("node", "dev"), None),
            P(None, "dev", "node"),
            P(None, "dev", "node"),
            P(None, "node", "dev"),
        ),
        check_vma=False,
    )
```

profile of v0, /device:TPU:0, one launch (start us, length us, event | category | flops | bytes accessed | tf_op | source)
XLA Modules:
  0.0 319.0 jit_solution(12823636620467152112)
XLA Ops:
  8.7 0.9 fusion.23
  10.5 0.8 fusion.24
  11.6 2.8 convolution_convert_fusion
  16.0 33.8 %all_to_all.40 = bf16[16,4,14464]{2,1,0:T(4,128)(2,1)} all-to-all(bf16[16,4,14464]{2,1,0:T(4,128)(2,1)S(1)} %bitcast.58), channel_id=1, replica_groups=mesh['node'=8,'dev'=16] {'dev'}, dimensions={0} | all-to-all | bytes 3702784 | tf_op jit(solution)/shard_map/all_to_all | solution.py:77
  49.8 2.8 reshape.139
  52.7 1.0 slice.114
  53.7 1.0 slice.109
  54.7 1.6 fusion.39
  56.3 1.3 pad_maximum_fusion.2
  57.7 3.7 %all-to-all-start.3 = ((bf16[16,448,128]{2,1,0:T(8,128)(2,1)}), bf16[16,448,128]{2,1,0:T(8,128)(2,1)S(1)}, u32[]{:S(2)}, u32[]{:S(2)}) async-start(bf16[16,448,128]{2,1,0:T(8,128)(2,1)} %bitcast.63), calls=%async_computation.3 | async-start | bytes 3670016 | tf_op jit(solution)/shard_map/all_to_all | solution.py:54
  61.4 1.8 fusion.37
  63.2 1.3 pad_maximum_fusion
  64.5 23.4 %all-to-all-done.3 = bf16[16,448,128]{2,1,0:T(8,128)(2,1)S(1)} async-done(((bf16[16,448,128]{2,1,0:T(8,128)(2,1)}), bf16[16,448,128]{2,1,0:T(8,128)(2,1)S(1)}, u32[]{:S(2)}, u32[]{:S(2)}) %all-to-all-start.3) | async-done | bytes 1835040 | tf_op jit(solution)/shard_map/all_to_all | solution.py:54
  88.0 4.4 %all-to-all-start.1 = ((bf16[16,448,128]{2,1,0:T(8,128)(2,1)}), bf16[16,448,128]{2,1,0:T(8,128)(2,1)}, u32[]{:S(2)}, u32[]{:S(2)}) async-start(bf16[16,448,128]{2,1,0:T(8,128)(2,1)} %bitcast.62), calls=%async_computation.1 | async-start | bytes 3670016 | tf_op jit(solution)/shard_map/all_to_all | solution.py:56
  92.4 1.6 fusion.38
  94.0 1.3 pad_maximum_fusion.1
  95.4 23.1 %all-to-all-done.1 = bf16[16,448,128]{2,1,0:T(8,128)(2,1)} async-done(((bf16[16,448,128]{2,1,0:T(8,128)(2,1)}), bf16[16,448,128]{2,1,0:T(8,128)(2,1)}, u32[]{:S(2)}, u32[]{:S(2)}) %all-to-all-start.1) | async-done | bytes 1835040 | tf_op jit(solution)/shard_map/all_to_all | solution.py:56
  118.5 4.4 %all-to-all-start.2 = ((bf16[16,448,128]{2,1,0:T(8,128)(2,1)}), bf16[16,448,128]{2,1,0:T(8,128)(2,1)}, u32[]{:S(2)}, u32[]{:S(2)}) async-start(bf16[16,448,128]{2,1,0:T(8,128)(2,1)} %bitcast.61), calls=%async_computation.2 | async-start | bytes 3670016 | tf_op jit(solution)/shard_map/all_to_all | solution.py:55
  123.2 5.8 %fusion.40 = f32[512,128]{0,1:T(8,128)S(1)} fusion(bf16[512,7168]{1,0:T(8,128)(2,1)} %all-gather.5.cloned.1.call-done, bf16[7168,128]{1,0:T(8,128)(2,1)S(1)} %bitcast.56), kind=kOutput, calls=%fused_computation.101 | convolution fusion | flops 939524096 | bytes 9437184 | tf_op jit(solution)/shard_map/dot_general | solution.py:83
  129.0 15.7 %all-gather.3.cloned.1.call-done = bf16[512,7296]{1,0:T(8,128)(2,1)} async-done(((bf16[64,7296]{1,0:T(8,128)(2,1)}), bf16[512,7296]{1,0:T(8,128)(2,1)}) %all-gather.3.cloned.1.call-update) | async-done | bytes 7471120 | tf_op jit(solution)/shard_map/all_gather | solution.py:80
  144.6 1.0 convert_reduce_fusion
  145.7 6.1 %fusion.2 = f32[512,128]{0,1:T(8,128)S(1)} fusion(bf16[7168,128]{1,0:T(8,128)(2,1)} %bitcast.5, bf16[512,7296]{1,0:T(8,128)(2,1)} %all-gather.3.cloned.1.call-done), kind=kOutput, calls=%fused_computation.9 | convolution fusion | flops 939524096 | bytes 9437184 | tf_op jit(solution)/shard_map/dot_general | solution.py:85
  151.8 6.2 %broadcast_select_fusion.1 = (bf16[512,128]{0,1:T(8,128)(2,1)S(1)}, bf16[512,128]{0,1:T(8,128)(2,1)S(1)}, bf16[512,128]{0,1:T(8,128)(2,1)S(1)}, bf16[512,128]{0,...) fusion(pred[512]{0:T(512)(128)(4,1)S(1)} %fusion.28, ...), kind=kOutput, calls=%fused_computation.62 | convolution fusion | flops 940834816 | bytes 10750464 | tf_op jit(solution)/shard_map/dot_general | solution.py:84
  158.1 2.1 fusion.8
  160.3 8.9 %select_add_fusion = f32[512,7296]{1,0:T(8,128)} fusion(f32[512,7296]{1,0:T(8,128)S(1)} %fusion.8, bf16[512,128]{0,1:T(8,128)(2,1)S(1)} %get-tuple-element.28, f32[512]{0:T(512)S(1)} %multiply_reduce_fusion, pred[7296]{0:T(1024)(128)(4,1)S(1)} %iota_compare_fusion.3, bf16[7168,128]{1,0:T(8,128)(2,1)} %bitcast.7), kind=kOutput, calls=%fused_computation | convolution fusion | flops 967507968 | bytes 31859840 | tf_op jit(solution)/shard_map/rh,dh->rd/dot_general | solution.py:117
  169.2 5.2 %convolution_reduce-precision_fusion = f32[7168,256]{1,0:T(8,128)S(1)} fusion(bf16[512,7296]{1,0:T(8,128)(2,1)} %all-gather.3.cloned.1.call-done, bf16[512,128]{0,1:T(8,128)(2,1)S(1)} %get-tuple-element.31, bf16[512,128]{0,1:T(8,128)(2,1)S(1)} %get-tuple-element.7), kind=kOutput, calls=%fused_computation.2 | convolution fusion | flops 1881407488 | bytes 14942208 | tf_op jit(solution)/shard_map/rd,rh->dh/dot_general | solution.py:106
  174.4 1.6 fusion.4
  176.0 7.0 %all-to-all-start.7 = ((bf16[16,448,128]{2,1,0:T(8,128)(2,1)}), bf16[16,448,128]{2,1,0:T(8,128)(2,1)S(1)}, u32[]{:S(2)}, u32[]{:S(2)}) async-start(bf16[16,448,128]{2,1,0:T(8,128)(2,1)} %bitcast.66), calls=%async_computation.8 | async-start | bytes 3670016 | tf_op jit(solution)/shard_map/all_to_all | solution.py:144
  183.0 5.3 %convolution_reduce-precision_fusion.2 = f32[7168,256]{1,0:T(8,128)S(1)} fusion(bf16[512,7168]{1,0:T(8,128)(2,1)} %all-gather.5.cloned.1.call-done, bf16[512,128]{0,1:T(8,128)(2,1)S(1)} %get-tuple-element.32, bf16[512,128]{0,1:T(8,128)(2,1)S(1)} %get-tuple-element.25), kind=kOutput, calls=%fused_computation.4 | convolution fusion | flops 1881407488 | bytes 14942208 | tf_op jit(solution)/shard_map/rd,rh->dh/dot_general | solution.py:106
  188.4 1.6 fusion.6
  189.9 22.3 %all-to-all-done.7 = bf16[16,448,128]{2,1,0:T(8,128)(2,1)S(1)} async-done(((bf16[16,448,128]{2,1,0:T(8,128)(2,1)}), bf16[16,448,128]{2,1,0:T(8,128)(2,1)S(1)}, u32[]{:S(2)}, u32[]{:S(2)}) %all-to-all-start.7) | async-done | bytes 1835040 | tf_op jit(solution)/shard_map/all_to_all | solution.py:144
  212.2 4.4 %all-to-all-start.5 = ((bf16[16,448,128]{2,1,0:T(8,128)(2,1)}), bf16[16,448,128]{2,1,0:T(8,128)(2,1)}, u32[]{:S(2)}, u32[]{:S(2)}) async-start(bf16[16,448,128]{2,1,0:T(8,128)(2,1)} %bitcast.64), calls=%async_computation.6 | async-start | bytes 3670016 | tf_op jit(solution)/shard_map/all_to_all | solution.py:139
  216.6 5.4 %convolution_reduce-precision_fusion.1 = f32[7168,256]{1,0:T(8,128)S(1)} fusion(bf16[512,7168]{1,0:T(8,128)(2,1)} %all-gather.5.cloned.1.call-done, bf16[512,128]{0,1:T(8,128)(2,1)S(1)} %get-tuple-element.33, bf16[512,128]{0,1:T(8,128)(2,1)S(1)} %get-tuple-element.27), kind=kOutput, calls=%fused_computation.3 | convolution fusion | flops 1881407488 | bytes 14942208 | tf_op jit(solution)/shard_map/rd,rh->dh/dot_general | solution.py:106
  222.0 1.6 fusion.5
  223.6 20.3 %all-to-all-done.5 = bf16[16,448,128]{2,1,0:T(8,128)(2,1)} async-done(((bf16[16,448,128]{2,1,0:T(8,128)(2,1)}), bf16[16,448,128]{2,1,0:T(8,128)(2,1)}, u32[]{:S(2)}, u32[]{:S(2)}) %all-to-all-start.5) | async-done | bytes 1835040 | tf_op jit(solution)/shard_map/all_to_all | solution.py:139
  243.9 3.7 %all-to-all-start.6 = ((bf16[16,448,128]{2,1,0:T(8,128)(2,1)}), bf16[16,448,128]{2,1,0:T(8,128)(2,1)S(1)}, u32[]{:S(2)}, u32[]{:S(2)}) async-start(bf16[16,448,128]{2,1,0:T(8,128)(2,1)} %bitcast.65), calls=%async_computation.7 | async-start | bytes 3670016 | tf_op jit(solution)/shard_map/all_to_all | solution.py:139
  247.6 5.5 %reduce-scatter.2.cloned.1.call-done = f32[64,7296]{1,0:T(8,128)} async-done(((f32[512,7296]{1,0:T(8,128)}), f32[64,7296]{1,0:T(8,128)}) %reduce-scatter.2.cloned.1.call-update) | async-done | bytes 1867792 | tf_op jit(solution)/shard_map/reduce_scatter | solution.py:122
  253.1 2.9 reshape.146
  255.9 18.5 %all-to-all-done.6 = bf16[16,448,128]{2,1,0:T(8,128)(2,1)S(1)} async-done(((bf16[16,448,128]{2,1,0:T(8,128)(2,1)}), bf16[16,448,128]{2,1,0:T(8,128)(2,1)S(1)}, u32[]{:S(2)}, u32[]{:S(2)}) %all-to-all-start.6) | async-done | bytes 1835040 | tf_op jit(solution)/shard_map/all_to_all | solution.py:139
  274.4 1.2 copy-done.1
  275.7 4.0 %all-to-all-start.4 = ((f32[16,4,7296]{2,1,0:T(4,128)}), f32[16,4,7296]{2,1,0:T(4,128)S(1)}, u32[]{:S(2)}, u32[]{:S(2)}) async-start(f32[16,4,7296]{2,1,0:T(4,128)} %reshape.146), calls=%async_computation.5 | async-start | bytes 3735552 | tf_op jit(solution)/shard_map/all_to_all | solution.py:123
  279.6 1.6 slice_bitcast_fusion.1
  281.3 1.4 pad_maximum_fusion.5
  282.7 1.6 slice_bitcast_fusion.5
  284.4 2.3 pad_maximum_fusion.3
  286.8 19.9 %all-to-all-done.4 = f32[16,4,7296]{2,1,0:T(4,128)S(1)} async-done(((f32[16,4,7296]{2,1,0:T(4,128)}), f32[16,4,7296]{2,1,0:T(4,128)S(1)}, u32[]{:S(2)}, u32[]{:S(2)}) %all-to-all-start.4) | async-done | bytes 1867808 | tf_op jit(solution)/shard_map/all_to_all | solution.py:123
  307.5 1.1 fusion.22
  309.5 3.0 fusion
  (45 shorter events, 6.5 us)
Async XLA Ops:
  7.2 116.0 %all-gather.5.cloned.1.call-start = ((), (), s32[]{:S(2)}) async-start(), calls=%async_computation.10 | async-start | bytes 8257536 | tf_op jit(solution)/shard_map/all_gather | solution.py:79
  8.4 6.0 %copy-start.3 = (bf16[256,7168]{1,0:T(8,128)(2,1)S(1)}, bf16[256,7168]{1,0:T(8,128)(2,1)}, u32[]{:S(2)}) copy-start(bf16[256,7168]{1,0:T(8,128)(2,1)} %param.8) | copy-start | bytes 11010052
  53.7 91.0 %all-gather.3.cloned.1.call-start = ((), (), s32[]{:S(2)}) async-start(), calls=%async_computation.9 | async-start | bytes 8404992 | tf_op jit(solution)/shard_map/all_gather | solution.py:80
  57.7 30.3 %all-to-all-start.3 = ((bf16[16,448,128]{2,1,0:T(8,128)(2,1)}), bf16[16,448,128]{2,1,0:T(8,128)(2,1)S(1)}, u32[]{:S(2)}, u32[]{:S(2)}) async-start(bf16[16,448,128]{2,1,0:T(8,128)(2,1)} %bitcast.63), calls=%async_computation.3 | async-start | bytes 3670016 | tf_op jit(solution)/shard_map/all_to_all | solution.py:54
  88.0 30.5 %all-to-all-start.1 = ((bf16[16,448,128]{2,1,0:T(8,128)(2,1)}), bf16[16,448,128]{2,1,0:T(8,128)(2,1)}, u32[]{:S(2)}, u32[]{:S(2)}) async-start(bf16[16,448,128]{2,1,0:T(8,128)(2,1)} %bitcast.62), calls=%async_computation.1 | async-start | bytes 3670016 | tf_op jit(solution)/shard_map/all_to_all | solution.py:56
  118.5 33.3 %all-to-all-start.2 = ((bf16[16,448,128]{2,1,0:T(8,128)(2,1)}), bf16[16,448,128]{2,1,0:T(8,128)(2,1)}, u32[]{:S(2)}, u32[]{:S(2)}) async-start(bf16[16,448,128]{2,1,0:T(8,128)(2,1)} %bitcast.61), calls=%async_computation.2 | async-start | bytes 3670016 | tf_op jit(solution)/shard_map/all_to_all | solution.py:55
  122.9 130.2 %reduce-scatter.2.cloned.1.call-start = ((), (), s32[]{:S(2)}) async-start(), calls=%async_computation.11 | async-start | bytes 16809984 | tf_op jit(solution)/shard_map/reduce_scatter | solution.py:122
  176.0 36.2 %all-to-all-start.7 = ((bf16[16,448,128]{2,1,0:T(8,128)(2,1)}), bf16[16,448,128]{2,1,0:T(8,128)(2,1)S(1)}, u32[]{:S(2)}, u32[]{:S(2)}) async-start(bf16[16,448,128]{2,1,0:T(8,128)(2,1)} %bitcast.66), calls=%async_computation.8 | async-start | bytes 3670016 | tf_op jit(solution)/shard_map/all_to_all | solution.py:144
  212.2 9.8 %copy-start = (bf16[16,448,128]{2,1,0:T(8,128)(2,1)}, bf16[16,448,128]{2,1,0:T(8,128)(2,1)S(1)}, u32[]{:S(2)}) copy-start(bf16[16,448,128]{2,1,0:T(8,128)(2,1)S(1)} %all-to-all-done.7) | copy-start | bytes 5505028
  212.2 31.7 %all-to-all-start.5 = ((bf16[16,448,128]{2,1,0:T(8,128)(2,1)}), bf16[16,448,128]{2,1,0:T(8,128)(2,1)}, u32[]{:S(2)}, u32[]{:S(2)}) async-start(bf16[16,448,128]{2,1,0:T(8,128)(2,1)} %bitcast.64), calls=%async_computation.6 | async-start | bytes 3670016 | tf_op jit(solution)/shard_map/all_to_all | solution.py:139
  243.9 30.5 %all-to-all-start.6 = ((bf16[16,448,128]{2,1,0:T(8,128)(2,1)}), bf16[16,448,128]{2,1,0:T(8,128)(2,1)S(1)}, u32[]{:S(2)}, u32[]{:S(2)}) async-start(bf16[16,448,128]{2,1,0:T(8,128)(2,1)} %bitcast.65), calls=%async_computation.7 | async-start | bytes 3670016 | tf_op jit(solution)/shard_map/all_to_all | solution.py:139
  274.4 1.2 copy-start.1
  275.7 31.0 %all-to-all-start.4 = ((f32[16,4,7296]{2,1,0:T(4,128)}), f32[16,4,7296]{2,1,0:T(4,128)S(1)}, u32[]{:S(2)}, u32[]{:S(2)}) async-start(f32[16,4,7296]{2,1,0:T(4,128)} %reshape.146), calls=%async_computation.5 | async-start | bytes 3735552 | tf_op jit(solution)/shard_map/all_to_all | solution.py:123
  281.2 3.0 copy-start.2
  307.5 1.3 copy-start.4
Sparse Core Ops, SparseCore 0:
  53.8 42.6 all-gather.4
  98.7 45.8 all-gather.2
  169.3 83.7 reduce-scatter.1
where the time goes:
time: 320 us; the launch traced here: 319 us
  waiting for transfers between devices  149 us (47%)
  matrix products  52.8 us (16%)
  blocking collectives  33.8 us (11%)
  starting transfers between devices  32 us (10%)
  other arithmetic  19.1 us (6%)
  local copies, waits for them, and re-layouts  18.5 us (6%)
  between operations  14.1 us (4%)
    all_to_all x2, waiting for transfers between devices, home(): lax.all_to_all(sent, 'dev', 0, 0, tiled=True)  38.8 us
    all_to_all x1, blocking collectives, local(): lax.all_to_all(both.reshape(col_count, per_rank, both_width), 'dev', 0, 0...  33.8 us
    all_to_all x1, waiting for transfers between devices, local(): lax.all_to_all(send_wg, 'dev', 0, 0, tiled=True).reshape(model_width, half)  23.4 us
    all_to_all x1, waiting for transfers between devices, local(): lax.all_to_all(send_wd, 'dev', 0, 0, tiled=True).reshape(model_width, half)  23.1 us
    all_to_all x1, waiting for transfers between devices, local(): lax.all_to_all(grad_down_cols.reshape(col_count, chunk, half), 'dev', 0,...  22.3 us
    all_to_all x1, waiting for transfers between devices, local(): lax.all_to_all(summed.reshape(col_count, per_rank, wide), 'dev', 0, 0, ti...  19.9 us
    dot_general x3, matrix products, slot_pair_sum(): jnp.einsum('rd,rh->dh', rows, by_slot(d), preferred_element_type=jnp.floa...  15.9 us
    all_gather x1, waiting for transfers between devices, local(): dy_ext = lax.all_gather(both[:, model_width:], 'node', axis=0, tiled=True)  15.7 us
  transfers between devices with their start and end apart: 10, of which 8 were waited for; matrix products, arithmetic and copies ran while one was open for 17% of the time, Pallas kernels for 0%

commit v1 on v0

--- a/solution.py
+++ b/solution.py
@@ -1,12 +1,37 @@
+import functools
 import jax
 import jax.numpy as jnp
 from jax import lax
 from jax.sharding import PartitionSpec as P
+from jax.lax import axis_index, axis_size, ppermute
 
 TOP = 8
 CAP = 2
 REPS = 2
 LANE = 128
+
+
+def choose_the_rates(mine_x, row_dim):
+    y_new, z2, known = (axis_size("node"), axis_index("node"), mine_x.shape[row_dim])
+    all_rows = [at * y_new if tick == row_dim else at for tick, at in enumerate(mine_x.shape)]
+    t1 = lax.dynamic_update_slice_in_dim(
+        jnp.zeros(all_rows, mine_x.dtype), mine_x, z2 * known, axis=row_dim
+    )
+    tmp = lower = mine_x
+    for i0 in range(1, y_new // 2 + 1):
+        tmp = ppermute(
+            tmp, "node", list(map(lambda tick: (tick, (tick + 1) % y_new), range(y_new)))
+        )
+        t1 = lax.dynamic_update_slice_in_dim(t1, tmp, (z2 - i0) % y_new * known, axis=row_dim)
+        if 2 * i0 < y_new:
+            lower = ppermute(
+                lower, "node", list(map(lambda tick: (tick, (tick - 1) % y_new), range(y_new)))
+            )
+            t1 = lax.dynamic_update_slice_in_dim(t1, lower, (z2 + i0) % y_new * known, axis=row_dim)
+    return t1
+
+
+use_turns_in = functools.partial(choose_the_rates, row_dim=0)
 
 
 def routing(expert_ids, slot_plan, slot_count, round_total):
@@ -77,7 +102,7 @@
     both = lax.all_to_all(both.reshape(col_count, per_rank, both_width), "dev", 0, 0, tiled=True)
     both = both.reshape(col_count * per_rank, both_width)
     x_rows = lax.all_gather(both[:, :model_width], "node", axis=0, tiled=True)
-    dy_ext = lax.all_gather(both[:, model_width:], "node", axis=0, tiled=True)
+    dy_ext = use_turns_in(both[:, model_width:])
     dy_rows = dy_ext[:, :model_width]
     gate_rows = dy_ext[:, model_width].astype(jnp.float32)[:, None]
     gate_pre = jnp.dot(x_rows, slot_gate, preferred_element_type=jnp.float32)

time: 320 us -> 511 us (1.60)
  the two profiles are of different devices: /device:TPU:0 before, /device:TPU:6 now
where the time goes in v1:
time: 511 us; the launch traced here: 505 us
  local copies, waits for them, and re-layouts  204 us (40%)
  waiting for transfers between devices  144 us (28%)
  matrix products  51 us (10%)
  starting transfers between devices  37.6 us (7%)
  blocking collectives  33.7 us (7%)
  other arithmetic  20.5 us (4%)
  between operations  14.5 us (3%)
    dynamic_update_slice x4, local copies, waits for them, and re-layouts, choose_the_rates(): lax.dynamic_update_slice_in_dim(t1, tmp, (z2 - i0) % y_new * known, axis=...  81.7 us
    dynamic_update_slice x3, local copies, waits for them, and re-layouts, choose_the_rates(): lax.dynamic_update_slice_in_dim(t1, lower, (z2 + i0) % y_new * known, axi...  61.9 us
    all_to_all x2, waiting for transfers between devices, home(): lax.all_to_all(sent, 'dev', 0, 0, tiled=True)  49.8 us
    ppermute x4, waiting for transfers between devices, choose_the_rates(): ppermute(tmp, 'node', list(map(lambda tick: (tick, (tick + 1) % y_new), r...  35.1 us
    all_to_all x1, blocking collectives, local(): lax.all_to_all(both.reshape(col_count, per_rank, both_width), 'dev', 0, 0...  33.7 us
    all_to_all x1, waiting for transfers between devices, local(): lax.all_to_all(grad_down_cols.reshape(col_count, chunk, half), 'dev', 0,...  21.8 us
    all_to_all x1, waiting for transfers between devices, local(): lax.all_to_all(summed.reshape(col_count, per_rank, wide), 'dev', 0, 0, ti...  20.8 us
    dynamic_update_slice x1, local copies, waits for them, and re-layouts, choose_the_rates(): lax.dynamic_update_slice_in_dim(jnp.zeros(all_rows, mine_x.dtype), mine_x...  18 us
  transfers between devices with their start and end apart: 16, of which 11 were waited for; matrix products, arithmetic and copies ran while one was open for 47% of the time, Pallas kernels for 0%

profile of v1, /device:TPU:6, one launch (start us, length us, event | category | flops | bytes accessed | tf_op | source)
XLA Modules:
  0.0 505.0 jit_solution(5759567112038671719)
XLA Ops:
  11.6 2.8 convolution_convert_fusion
  16.0 33.7 %all_to_all.40 = bf16[16,4,14464]{2,1,0:T(4,128)(2,1)} all-to-all(bf16[16,4,14464]{2,1,0:T(4,128)(2,1)S(1)} %bitcast.59), channel_id=1, replica_groups=mesh['node'=8,'dev'=16] {'dev'}, dimensions={0} | all-to-all | bytes 3702784 | tf_op jit(solution)/shard_map/all_to_all | solution.py:102
  49.7 3.9 reshape.139
  53.6 2.2 slice.114
  59.2 4.4 all-to-all-start.1
  65.4 16.5 %collective-permute-done = bf16[64,7296]{1,0:T(8,128)(2,1)} collective-permute-done((bf16[64,7296]{1,0:T(8,128)(2,1)S(1)}, bf16[64,7296]{1,0:T(8,128)(2,1)}, u32[]{:S(2)}, u32[]{:S(2)}) %collective-permute-start) | collective-permute-done | bytes 933920 | tf_op jit(solution)/shard_map/ppermute | solution.py:22
  84.8 10.0 %all-to-all-done.1 = bf16[16,448,128]{2,1,0:T(8,128)(2,1)} async-done(((bf16[16,448,128]{2,1,0:T(8,128)(2,1)}), bf16[16,448,128]{2,1,0:T(8,128)(2,1)}, u32[]{:S(2)}, u32[]{:S(2)}) %all-to-all-start.1) | async-done | bytes 1835040 | tf_op jit(solution)/shard_map/all_to_all | solution.py:81
  94.8 3.7 all-to-all-start.3
  99.2 11.3 %collective-permute-done.2 = bf16[64,7296]{1,0:T(8,128)(2,1)} collective-permute-done((bf16[64,7296]{1,0:T(8,128)(2,1)}, bf16[64,7296]{1,0:T(8,128)(2,1)}, u32[]{:S(2)}, u32[]{:S(2)}) %collective-permute-start.2) | collective-permute-done | bytes 933920 | tf_op jit(solution)/shard_map/ppermute | solution.py:22
  110.5 3.7 collective-permute-done.3
  114.2 2.2 collective-permute-start.5
  116.4 7.4 %collective-permute-done.4 = bf16[64,7296]{1,0:T(8,128)(2,1)} collective-permute-done((bf16[64,7296]{1,0:T(8,128)(2,1)}, bf16[64,7296]{1,0:T(8,128)(2,1)}, u32[]{:S(2)}, u32[]{:S(2)}) %collective-permute-start.4) | collective-permute-done | bytes 933920 | tf_op jit(solution)/shard_map/ppermute | solution.py:22
  127.0 4.4 all-to-all-start.2
  133.4 3.5 broadcast_in_dim.177
  136.9 18.0 %dynamic_update_slice.24 = bf16[512,7296]{0,1:T(8,128)(2,1)} dynamic-update-slice(bf16[512,7296]{0,1:T(8,128)(2,1)} %broadcast_in_dim.177, bf16[64,7296]{0,1:T(8,128)(2,1)} %copy.37, s32[]{:T(128)S(6)} %select_n.127, s32[]{:T(128)} %constant.79.clone.1) | dynamic-update-slice | bytes 1867780 | tf_op jit(solution)/shard_map/dynamic_update_slice | solution.py:17
  154.9 2.7 copy.38
  157.5 21.9 %dynamic_update_slice.25 = bf16[512,7296]{0,1:T(8,128)(2,1)} dynamic-update-slice(bf16[512,7296]{0,1:T(8,128)(2,1)} %dynamic_update_slice.24, bf16[64,7296]{0,1:T(8,128)(2,1)} %copy.38, s32[]{:T(128)S(6)} %select_n.129, s32[]{:T(128)} %constant.79.clone.1) | dynamic-update-slice | bytes 1867780 | tf_op jit(solution)/shard_map/dynamic_update_slice | solution.py:25
  179.5 2.6 copy.39
  182.1 21.1 %dynamic_update_slice.26 = bf16[512,7296]{0,1:T(8,128)(2,1)} dynamic-update-slice(bf16[512,7296]{0,1:T(8,128)(2,1)} %dynamic_update_slice.25, bf16[64,7296]{0,1:T(8,128)(2,1)} %copy.39, s32[]{:T(128)S(6)} %select_n.131, s32[]{:T(128)} %constant.79.clone.1) | dynamic-update-slice | bytes 1867780 | tf_op jit(solution)/shard_map/dynamic_update_slice | solution.py:30
  203.2 2.7 copy.40
  205.9 18.9 %dynamic_update_slice.27 = bf16[512,7296]{0,1:T(8,128)(2,1)} dynamic-update-slice(bf16[512,7296]{0,1:T(8,128)(2,1)} %dynamic_update_slice.26, bf16[64,7296]{0,1:T(8,128)(2,1)} %copy.40, s32[]{:T(128)S(6)} %select_n.133, s32[]{:T(128)} %constant.79.clone.1) | dynamic-update-slice | bytes 1867780 | tf_op jit(solution)/shard_map/dynamic_update_slice | solution.py:25
  224.8 2.6 copy.41
  227.4 18.9 %dynamic_update_slice.28 = bf16[512,7296]{0,1:T(8,128)(2,1)} dynamic-update-slice(bf16[512,7296]{0,1:T(8,128)(2,1)} %dynamic_update_slice.27, bf16[64,7296]{0,1:T(8,128)(2,1)} %copy.41, s32[]{:T(128)S(6)} %select_n.135, s32[]{:T(128)} %constant.79.clone.1) | dynamic-update-slice | bytes 1867780 | tf_op jit(solution)/shard_map/dynamic_update_slice | solution.py:30
  246.4 2.6 copy.42
  249.0 21.9 %dynamic_update_slice.29 = bf16[512,7296]{0,1:T(8,128)(2,1)} dynamic-update-slice(bf16[512,7296]{0,1:T(8,128)(2,1)} %dynamic_update_slice.28, bf16[64,7296]{0,1:T(8,128)(2,1)} %copy.42, s32[]{:T(128)S(6)} %select_n.137, s32[]{:T(128)} %constant.79.clone.1) | dynamic-update-slice | bytes 1867780 | tf_op jit(solution)/shard_map/dynamic_update_slice | solution.py:25
  270.9 2.6 copy.43
  273.6 21.9 %dynamic_update_slice.30 = bf16[512,7296]{0,1:T(8,128)(2,1)} dynamic-update-slice(bf16[512,7296]{0,1:T(8,128)(2,1)} %dynamic_update_slice.29, bf16[64,7296]{0,1:T(8,128)(2,1)} %copy.43, s32[]{:T(128)S(6)} %select_n.139, s32[]{:T(128)} %constant.79.clone.1) | dynamic-update-slice | bytes 1867780 | tf_op jit(solution)/shard_map/dynamic_update_slice | solution.py:30
  295.5 2.6 copy.44
  298.2 18.9 %dynamic_update_slice.31 = bf16[512,7296]{0,1:T(8,128)(2,1)} dynamic-update-slice(bf16[512,7296]{0,1:T(8,128)(2,1)} %dynamic_update_slice.30, bf16[64,7296]{0,1:T(8,128)(2,1)} %copy.44, s32[]{:T(128)S(6)} %select_n.141, s32[]{:T(128)} %constant.79.clone.1) | dynamic-update-slice | bytes 1867780 | tf_op jit(solution)/shard_map/dynamic_update_slice | solution.py:25
  317.7 4.8 fusion.2
  322.6 5.6 %fusion.40 = f32[512,128]{0,1:T(8,128)S(1)} fusion(bf16[512,7168]{1,0:T(8,128)(2,1)} %all-gather.2.cloned.1.call-done, bf16[7168,128]{1,0:T(8,128)(2,1)S(1)} %bitcast.57), kind=kOutput, calls=%fused_computation.101 | convolution fusion | flops 939524096 | bytes 9437184 | tf_op jit(solution)/shard_map/dot_general | solution.py:108
  328.2 6.2 %broadcast_select_fusion.1 = (bf16[512,128]{0,1:T(8,128)(2,1)S(1)}, bf16[512,128]{0,1:T(8,128)(2,1)S(1)}, bf16[512,128]{0,1:T(8,128)(2,1)S(1)}, bf16[512,128]{0,...) fusion(pred[512]{0:T(512)(128)(4,1)S(1)} %fusion.28, ...), kind=kOutput, calls=%fused_computation.61 | convolution fusion | flops 940834816 | bytes 10750464 | tf_op jit(solution)/shard_map/dot_general | solution.py:109
  334.6 2.1 fusion.8
  336.7 8.7 %select_add_fusion = f32[512,7296]{1,0:T(8,128)} fusion(f32[512,7296]{1,0:T(8,128)S(1)} %fusion.8, bf16[512,128]{0,1:T(8,128)(2,1)S(1)} %get-tuple-element.28, f32[512]{0:T(512)S(1)} %multiply_reduce_fusion, pred[7296]{0:T(1024)(128)(4,1)S(1)} %iota_compare_fusion.3, bf16[7168,128]{1,0:T(8,128)(2,1)} %bitcast.8), kind=kOutput, calls=%fused_computation | convolution fusion | flops 967507968 | bytes 31859840 | tf_op jit(solution)/shard_map/rh,dh->rd/dot_general | solution.py:142
  345.4 5.2 %convolution_reduce-precision_fusion = f32[7168,256]{1,0:T(8,128)S(1)} fusion(bf16[512,7296]{0,1:T(8,128)(2,1)} %dynamic_update_slice.31, bf16[512,128]{0,1:T(8,128)(2,1)S(1)} %get-tuple-element.31, bf16[512,128]{0,1:T(8,128)(2,1)S(1)} %get-tuple-element.7), kind=kOutput, calls=%fused_computation.2 | convolution fusion | flops 1881407488 | bytes 14942208 | tf_op jit(solution)/shard_map/rd,rh->dh/dot_general | solution.py:131
  352.2 7.1 %all-to-all-start.7 = ((bf16[16,448,128]{2,1,0:T(8,128)(2,1)}), bf16[16,448,128]{2,1,0:T(8,128)(2,1)S(1)}, u32[]{:S(2)}, u32[]{:S(2)}) async-start(bf16[16,448,128]{2,1,0:T(8,128)(2,1)} %bitcast.65), calls=%async_computation.8 | async-start | bytes 3670016 | tf_op jit(solution)/shard_map/all_to_all | solution.py:169
  359.3 5.2 %convolution_reduce-precision_fusion.1 = f32[7168,256]{1,0:T(8,128)S(1)} fusion(bf16[512,7168]{1,0:T(8,128)(2,1)} %all-gather.2.cloned.1.call-done, bf16[512,128]{0,1:T(8,128)(2,1)S(1)} %get-tuple-element.33, bf16[512,128]{0,1:T(8,128)(2,1)S(1)} %get-tuple-element.27), kind=kOutput, calls=%fused_computation.3 | convolution fusion | flops 1881407488 | bytes 14942208 | tf_op jit(solution)/shard_map/rd,rh->dh/dot_general | solution.py:131
  366.2 21.8 %all-to-all-done.7 = bf16[16,448,128]{2,1,0:T(8,128)(2,1)S(1)} async-done(((bf16[16,448,128]{2,1,0:T(8,128)(2,1)}), bf16[16,448,128]{2,1,0:T(8,128)(2,1)S(1)}, u32[]{:S(2)}, u32[]{:S(2)}) %all-to-all-start.7) | async-done | bytes 1835040 | tf_op jit(solution)/shard_map/all_to_all | solution.py:169
  387.9 4.4 all-to-all-start.6
  392.4 5.4 %convolution_reduce-precision_fusion.2 = f32[7168,256]{1,0:T(8,128)S(1)} fusion(bf16[512,7168]{1,0:T(8,128)(2,1)} %all-gather.2.cloned.1.call-done, bf16[512,128]{0,1:T(8,128)(2,1)S(1)} %get-tuple-element.32, bf16[512,128]{0,1:T(8,128)(2,1)S(1)} %get-tuple-element.25), kind=kOutput, calls=%fused_computation.4 | convolution fusion | flops 1881407488 | bytes 14942208 | tf_op jit(solution)/shard_map/rd,rh->dh/dot_general | solution.py:131
  399.3 24.7 %all-to-all-done.6 = bf16[16,448,128]{2,1,0:T(8,128)(2,1)} async-done(((bf16[16,448,128]{2,1,0:T(8,128)(2,1)}), bf16[16,448,128]{2,1,0:T(8,128)(2,1)}, u32[]{:S(2)}, u32[]{:S(2)}) %all-to-all-start.6) | async-done | bytes 1835040 | tf_op jit(solution)/shard_map/all_to_all | solution.py:164
  424.0 4.4 all-to-all-start.5
  430.5 2.9 reshape.146
  433.4 25.1 %all-to-all-done.5 = bf16[16,448,128]{2,1,0:T(8,128)(2,1)} async-done(((bf16[16,448,128]{2,1,0:T(8,128)(2,1)}), bf16[16,448,128]{2,1,0:T(8,128)(2,1)}, u32[]{:S(2)}, u32[]{:S(2)}) %all-to-all-start.5) | async-done | bytes 1835040 | tf_op jit(solution)/shard_map/all_to_all | solution.py:164
  458.4 4.4 all-to-all-start.4
  467.6 2.3 pad_maximum_fusion.3
  470.0 20.8 %all-to-all-done.4 = f32[16,4,7296]{2,1,0:T(4,128)} async-done(((f32[16,4,7296]{2,1,0:T(4,128)}), f32[16,4,7296]{2,1,0:T(4,128)}, u32[]{:S(2)}, u32[]{:S(2)}) %all-to-all-start.4) | async-done | bytes 1867808 | tf_op jit(solution)/shard_map/all_to_all | solution.py:148
  494.4 3.0 fusion
  (69 shorter events, 36.8 us)
Async XLA Ops:
  7.2 315.4 %all-gather.2.cloned.1.call-start = ((), (), s32[]{:S(2)}) async-start(), calls=%async_computation.9 | async-start | bytes 8257536 | tf_op jit(solution)/shard_map/all_gather | solution.py:104
  8.4 6.0 %copy-start.1 = (bf16[256,7168]{1,0:T(8,128)(2,1)S(1)}, bf16[256,7168]{1,0:T(8,128)(2,1)}, u32[]{:S(2)}) copy-start(bf16[256,7168]{1,0:T(8,128)(2,1)} %param.8) | copy-start | bytes 11010052
  55.7 2.1 copy-start
  57.9 24.0 %collective-permute-start = (bf16[64,7296]{1,0:T(8,128)(2,1)S(1)}, bf16[64,7296]{1,0:T(8,128)(2,1)}, u32[]{:S(2)}, u32[]{:S(2)}) collective-permute-start(bf16[64,7296]{1,0:T(8,128)(2,1)S(1)} %slice.109), channel_id=1, source_target_pairs={{0,16},{16,32},{32,48},{48,64},{64,80},{80,96},{96,112},{112,0},{1... | collective-permute-start | bytes 2801672 | tf_op jit(solution)/shard_map/ppermute | solution.py:22
  59.2 35.6 %all-to-all-start.1 = ((bf16[16,448,128]{2,1,0:T(8,128)(2,1)}), bf16[16,448,128]{2,1,0:T(8,128)(2,1)}, u32[]{:S(2)}, u32[]{:S(2)}) async-start(bf16[16,448,128]{2,1,0:T(8,128)(2,1)} %bitcast.5), calls=%async_computation.1 | async-start | bytes 3670016 | tf_op jit(solution)/shard_map/all_to_all | solution.py:81
  63.7 34.9 %collective-permute-start.1 = (bf16[64,7296]{1,0:T(8,128)(2,1)S(1)}, bf16[64,7296]{1,0:T(8,128)(2,1)}, u32[]{:S(2)}, u32[]{:S(2)}) collective-permute-start(bf16[64,7296]{1,0:T(8,128)(2,1)S(1)} %slice.109), channel_id=1, source_target_pairs={{0,112},{16,0},{32,16},{48,32},{64,48},{80,64},{96,80},{112,96},{1... | collective-permute-start | bytes 2801672 | tf_op jit(solution)/shard_map/ppermute | solution.py:27
  81.9 28.6 %collective-permute-start.2 = (bf16[64,7296]{1,0:T(8,128)(2,1)}, bf16[64,7296]{1,0:T(8,128)(2,1)}, u32[]{:S(2)}, u32[]{:S(2)}) collective-permute-start(bf16[64,7296]{1,0:T(8,128)(2,1)} %collective-permute-done), channel_id=1, source_target_pairs={{0,16},{16,32},{32,48},{48,64},{64,80},{80,96},{96,112},{112,0},{1... | collective-permute-start | bytes 2801672 | tf_op jit(solution)/shard_map/ppermute | solution.py:22
  94.8 32.2 %all-to-all-start.3 = ((bf16[16,448,128]{2,1,0:T(8,128)(2,1)}), bf16[16,448,128]{2,1,0:T(8,128)(2,1)S(1)}, u32[]{:S(2)}, u32[]{:S(2)}) async-start(bf16[16,448,128]{2,1,0:T(8,128)(2,1)} %bitcast.62), calls=%async_computation.3 | async-start | bytes 3670016 | tf_op jit(solution)/shard_map/all_to_all | solution.py:79
  98.5 15.7 %collective-permute-start.3 = (bf16[64,7296]{1,0:T(8,128)(2,1)}, bf16[64,7296]{1,0:T(8,128)(2,1)}, u32[]{:S(2)}, u32[]{:S(2)}) collective-permute-start(bf16[64,7296]{1,0:T(8,128)(2,1)} %collective-permute-done.1), channel_id=1, source_target_pairs={{0,112},{16,0},{32,16},{48,32},{64,48},{80,64},{96,80},{112,96},{1... | collective-permute-start | bytes 2801672 | tf_op jit(solution)/shard_map/ppermute | solution.py:27
  110.5 13.3 %collective-permute-start.4 = (bf16[64,7296]{1,0:T(8,128)(2,1)}, bf16[64,7296]{1,0:T(8,128)(2,1)}, u32[]{:S(2)}, u32[]{:S(2)}) collective-permute-start(bf16[64,7296]{1,0:T(8,128)(2,1)} %collective-permute-done.2), channel_id=1, source_target_pairs={{0,16},{16,32},{32,48},{48,64},{64,80},{80,96},{96,112},{112,0},{1... | collective-permute-start | bytes 2801672 | tf_op jit(solution)/shard_map/ppermute | solution.py:22
  114.2 156.7 %collective-permute-start.5 = (bf16[64,7296]{1,0:T(8,128)(2,1)}, bf16[64,7296]{1,0:T(8,128)(2,1)}, u32[]{:S(2)}, u32[]{:S(2)}) collective-permute-start(bf16[64,7296]{1,0:T(8,128)(2,1)} %collective-permute-done.3), channel_id=1, source_target_pairs={{0,112},{16,0},{32,16},{48,32},{64,48},{80,64},{96,80},{112,96},{1... | collective-permute-start | bytes 2801672 | tf_op jit(solution)/shard_map/ppermute | solution.py:27
  123.8 171.7 %collective-permute-start.6 = (bf16[64,7296]{1,0:T(8,128)(2,1)}, bf16[64,7296]{1,0:T(8,128)(2,1)}, u32[]{:S(2)}, u32[]{:S(2)}) collective-permute-start(bf16[64,7296]{1,0:T(8,128)(2,1)} %collective-permute-done.4), channel_id=1, source_target_pairs={{0,16},{16,32},{32,48},{48,64},{64,80},{80,96},{96,112},{112,0},{1... | collective-permute-start | bytes 2801672 | tf_op jit(solution)/shard_map/ppermute | solution.py:22
  127.0 201.2 %all-to-all-start.2 = ((bf16[16,448,128]{2,1,0:T(8,128)(2,1)}), bf16[16,448,128]{2,1,0:T(8,128)(2,1)}, u32[]{:S(2)}, u32[]{:S(2)}) async-start(bf16[16,448,128]{2,1,0:T(8,128)(2,1)} %bitcast.60), calls=%async_computation.2 | async-start | bytes 3670016 | tf_op jit(solution)/shard_map/all_to_all | solution.py:80
  131.4 299.1 %reduce-scatter.2.cloned.1.call-start = ((), (), s32[]{:S(2)}) async-start(), calls=%async_computation.10 | async-start | bytes 16809984 | tf_op jit(solution)/shard_map/reduce_scatter | solution.py:147
  352.2 35.7 %all-to-all-start.7 = ((bf16[16,448,128]{2,1,0:T(8,128)(2,1)}), bf16[16,448,128]{2,1,0:T(8,128)(2,1)S(1)}, u32[]{:S(2)}, u32[]{:S(2)}) async-start(bf16[16,448,128]{2,1,0:T(8,128)(2,1)} %bitcast.65), calls=%async_computation.8 | async-start | bytes 3670016 | tf_op jit(solution)/shard_map/all_to_all | solution.py:169
  387.9 36.1 %all-to-all-start.6 = ((bf16[16,448,128]{2,1,0:T(8,128)(2,1)}), bf16[16,448,128]{2,1,0:T(8,128)(2,1)}, u32[]{:S(2)}, u32[]{:S(2)}) async-start(bf16[16,448,128]{2,1,0:T(8,128)(2,1)} %bitcast.63), calls=%async_computation.7 | async-start | bytes 3670016 | tf_op jit(solution)/shard_map/all_to_all | solution.py:164
  424.0 34.4 %all-to-all-start.5 = ((bf16[16,448,128]{2,1,0:T(8,128)(2,1)}), bf16[16,448,128]{2,1,0:T(8,128)(2,1)}, u32[]{:S(2)}, u32[]{:S(2)}) async-start(bf16[16,448,128]{2,1,0:T(8,128)(2,1)} %bitcast.64), calls=%async_computation.6 | async-start | bytes 3670016 | tf_op jit(solution)/shard_map/all_to_all | solution.py:164
  458.4 32.3 %all-to-all-start.4 = ((f32[16,4,7296]{2,1,0:T(4,128)}), f32[16,4,7296]{2,1,0:T(4,128)}, u32[]{:S(2)}, u32[]{:S(2)}) async-start(f32[16,4,7296]{2,1,0:T(4,128)} %reshape.146), calls=%async_computation.5 | async-start | bytes 3735552 | tf_op jit(solution)/shard_map/all_to_all | solution.py:148
  494.4 3.1 copy-start.2
Sparse Core Ops, SparseCore 0:
  55.9 53.8 all-gather.1
  345.5 84.9 reduce-scatter.1
